TPU v7x, 256 devices: a whole 4x4x8 slice. The times are simulated.
256 devices in a mesh: req: 32 (over y, z), vocab: 8 (over x, core).
Axes of the slice: x: 4, y: 4, z: 8, core: 2. Of those that a mesh axis runs over, the one named last changes fastest.
Arguments:
- draft_states: bfloat16 [64, 64, 1536], P('req')
- parents: int32 [64, 64], P('req'), may hold values from -1 to 62, as said below
- live_draft_count: int32 [64], replicated, may hold values from 32 to 64, as said below
- path_index: int32 [64, 8], P('req'), may hold values from 0 to 63, as said below
- cached_length_list: int32 [64], P('req'), may hold values from 256 to 1792, as said below
- cached_key_rows: bfloat16 [65536, 768], P('req', 'vocab')
- cached_value_rows: bfloat16 [65536, 768], P('req', 'vocab'), may hold values from -6 to 6
- attend_gain: bfloat16 [1536], replicated, may hold values from 0.099609375 to 1.8984375
- hidden_gain: bfloat16 [1536], replicated, may hold values from 0.099609375 to 1.8984375
- final_gain: bfloat16 [1536], replicated, may hold values from 0.099609375 to 1.8984375
- query_weight: bfloat16 [1536, 1536], P(None, 'vocab')
- key_matrix: bfloat16 [1536, 768], P(None, 'vocab')
- value_matrix: bfloat16 [1536, 768], P(None, 'vocab'), may hold values from -0.15625 to 0.15625
- out_weight: bfloat16 [1536, 1536], P('vocab'), may hold values from -0.15625 to 0.15625
- gate_weight: bfloat16 [1536, 4096], P(None, 'vocab'), may hold values from -0.15625 to 0.15625
- up_weight: bfloat16 [1536, 4096], P(None, 'vocab'), may hold values from -0.15625 to 0.15625
- down_weight: bfloat16 [4096, 1536], P('vocab'), may hold values from -0.09375 to 0.09375
- head_weight: bfloat16 [1536, 32000], P(None, 'req'), may hold values from -0.4375 to 0.4375
Outputs:
- layer_output_rows: bfloat16 [64, 64, 1536], P('req', None, 'vocab')
- accepted_keys: bfloat16 [64, 8, 768], P('req', None, 'vocab')
- accepted_values: bfloat16 [64, 8, 768], P('req', None, 'vocab')
- norm_values: float32 [64, 8], P('req', 'vocab')
- maxima: float32 [64, 8], P(None, 'vocab')
Inputs may be any that keep to these rules, and one draw needn't show every extreme that they name: `live_draft_count`: the counts of all requests sum to exactly 3072. `parents`: each draft token's parent lies below its own index; the first token's is -1. `path_index`: each row lists 8 live draft tokens of its request, each the parent of the next. `cached_length_list`: the lengths of the 2 requests of one index of req sum to at most 2048, and to exactly 2048 on a quarter of the indices of req (at least one); on such an index one request is long and the others hold 256 each.
All inputs are finite; a program needn't handle non-finite values.
Results may differ from a plain program's by a relative error of at most 0.012.
Values may be sent and summed in bfloat16 or wider, within the bound.
No kernel may reach another device: no remote copies, remote signals or barrier semaphores. Data moves between devices by JAX's collectives and lax.ppermute only.
A program may use at most 64 MiB of HBM per device.

v0:
```python
import jax
import jax.numpy as jnp
from jax import lax
from jax.sharding import PartitionSpec as P

HEAD_SIZE = 96
eps_norm = 1e-05
rope_base = 100000.0
masked_score = -1e30


def apply_rotation(values, token_positions):
    half_dim = values.shape[-1] // 2
    inverse = rope_base ** (-jnp.arange(half_dim, dtype=jnp.float32) * 2.0 / values.shape[-1])
    angles = token_positions.astype(jnp.float32)[:, None] * inverse[None, :]
    cosine = jnp.cos(angles)[:, None, :]
    sine_of = jnp.sin(angles)[:, None, :]
    first_half = values[..., :half_dim]
    second_half = values[..., half_dim:]
    return jnp.concatenate(
        [first_half * cosine - second_half * sine_of, second_half * cosine + first_half * sine_of],
        axis=-1,
    )


def ancestors(parents):
    draft_length = parents.shape[-1]
    columns = jnp.arange(draft_length, dtype=jnp.int32)
    reached = jnp.eye(draft_length, dtype=jnp.float32) + (parents[..., :, None] == columns).astype(
        jnp.float32
    )
    for sweep_number in range((draft_length - 1).bit_length()):
        reached = jnp.minimum(
            jnp.einsum("bij,bjk->bik", reached, reached, precision=lax.Precision.HIGHEST), 1.0
        )
    return reached


def lookup(entries, indices):
    matches = indices[:, None] == jnp.arange(entries.shape[0], dtype=jnp.int32)[None, :]
    return jnp.sum(jnp.where(matches, entries[None, :], 0), axis=1)


def span_scores(query_block, first, last, number, joined_keys, block_len):
    pool_rows = joined_keys.shape[0]
    nominal = first + number * block_len
    actual = jnp.minimum(nominal, pool_rows - block_len)
    keys_block = lax.dynamic_slice_in_dim(joined_keys, actual, block_len, 0)
    scores = jnp.einsum(
        "kqd,pkd->kqp", query_block, keys_block, preferred_element_type=jnp.float32
    ) * query_block.shape[-1] ** (-0.5)
    slots = actual + jnp.arange(block_len, dtype=jnp.int32)
    allowed = (slots >= nominal) & (slots < jnp.minimum(last, nominal + block_len))
    return (scores, allowed[None, None, :], actual)


def span_max(query_block, first, last, joined_keys, block_len):
    block_count = (last - first + block_len - 1) // block_len

    def step(number, running):
        scores, allowed, actual = span_scores(
            query_block, first, last, number, joined_keys, block_len
        )
        return jnp.maximum(running, jnp.max(jnp.where(allowed, scores, masked_score), axis=2))

    start_max = jnp.full(query_block.shape[:2], masked_score, jnp.float32)
    return lax.fori_loop(0, block_count, step, start_max)


def span_sums(query_block, first, last, top, joined_keys, joined_values, block_len):
    block_count = (last - first + block_len - 1) // block_len

    def step(number, running):
        totals_now, weighted_now = running
        scores, allowed, actual = span_scores(
            query_block, first, last, number, joined_keys, block_len
        )
        weights = jnp.where(allowed, jnp.exp(scores - top[:, :, None]), 0.0).astype(jnp.bfloat16)
        values_block = lax.dynamic_slice_in_dim(joined_values, actual, block_len, 0)
        return (
            totals_now + jnp.sum(weights.astype(jnp.float32), axis=2),
            weighted_now
            + jnp.einsum("kqp,pkd->kqd", weights, values_block, preferred_element_type=jnp.float32),
        )

    start_sums = (
        jnp.zeros(query_block.shape[:2], jnp.float32),
        jnp.zeros(query_block.shape, jnp.float32),
    )
    return lax.fori_loop(0, block_count, step, start_sums)


def maxima_over(query_sets, firsts, lasts, joined_keys, block_len):
    return lax.map(
        lambda item: span_max(item[0], item[1], item[2], joined_keys, block_len),
        (query_sets, firsts, lasts),
    )


def sums_over(query_sets, firsts, lasts, tops, joined_keys, joined_values, block_len):
    return lax.map(
        lambda item: span_sums(
            item[0], item[1], item[2], item[3], joined_keys, joined_values, block_len
        ),
        (query_sets, firsts, lasts, tops),
    )


def feed_forward(hidden_in, gate_weight, up_weight, down_weight):
    gate_out = jnp.dot(hidden_in, gate_weight, preferred_element_type=jnp.float32)
    up_out = jnp.dot(hidden_in, up_weight, preferred_element_type=jnp.float32)
    hidden = (jax.nn.silu(gate_out) * up_out).astype(jnp.bfloat16)
    partial_sum = jnp.dot(hidden, down_weight, preferred_element_type=jnp.float32)
    summed = lax.psum(partial_sum.astype(jnp.bfloat16), "vocab")
    return summed


def per_device(
    draft_states,
    parents,
    live_draft_count,
    path_index,
    cached_length_list,
    cached_key_rows,
    cached_value_rows,
    attend_gain,
    hidden_gain,
    final_gain,
    query_weight,
    key_matrix,
    value_matrix,
    out_weight,
    gate_weight,
    up_weight,
    down_weight,
    head_weight,
):
    local_requests, draft_length, model_width = draft_states.shape
    token_rows = local_requests * draft_length
    request_shards = lax.axis_size("req")
    request_shard = lax.axis_index("req")
    vocab_shards = lax.axis_size("vocab")
    vocab_shard = lax.axis_index("vocab")
    head_dim = HEAD_SIZE
    key_local = key_matrix.shape[1] // head_dim
    query_local = query_weight.shape[1] // head_dim
    group_factor = query_local // key_local
    pool_rows = cached_key_rows.shape[0]
    rows_per_request = draft_length * group_factor
    states = draft_states.reshape(token_rows, model_width).astype(jnp.float32)
    normalized_states = (
        states
        * lax.rsqrt(jnp.mean(states * states, axis=1, keepdims=True) + eps_norm)
        * attend_gain.astype(jnp.float32)
    ).astype(jnp.bfloat16)
    reached = ancestors(parents)
    token_positions = (
        cached_length_list[:, None] + (jnp.sum(reached, axis=2) - 1.0).astype(jnp.int32)
    ).reshape(token_rows)
    query_vectors = apply_rotation(
        jnp.dot(normalized_states, query_weight, preferred_element_type=jnp.float32).reshape(
            token_rows, query_local, head_dim
        ),
        token_positions,
    ).astype(jnp.bfloat16)
    fresh_keys = apply_rotation(
        jnp.dot(normalized_states, key_matrix, preferred_element_type=jnp.float32).reshape(
            token_rows, key_local, head_dim
        ),
        token_positions,
    ).astype(jnp.bfloat16)
    fresh_values = (
        jnp.dot(normalized_states, value_matrix, preferred_element_type=jnp.float32)
        .astype(jnp.bfloat16)
        .reshape(token_rows, key_local, head_dim)
    )
    query_rows = (
        query_vectors.reshape(token_rows, key_local, group_factor, head_dim)
        .transpose(1, 0, 2, 3)
        .reshape(key_local, token_rows * group_factor, head_dim)
    )
    score_scale = head_dim ** (-0.5)
    same_request = jnp.eye(local_requests, dtype=jnp.float32)
    tree_mask = (
        jnp.einsum("jk,jim->jikm", same_request, reached).reshape(token_rows, token_rows) > 0.5
    )
    tree_mask = jnp.repeat(tree_mask, group_factor, axis=0)[None]
    tree_scores = (
        jnp.einsum("kqd,rkd->kqr", query_rows, fresh_keys, preferred_element_type=jnp.float32)
        * score_scale
    )
    tree_max = jnp.max(jnp.where(tree_mask, tree_scores, masked_score), axis=2)
    tree_top = tree_max.reshape(key_local, local_requests, rows_per_request).transpose(1, 0, 2)
    cache_end = jnp.cumsum(cached_length_list)
    cache_start = cache_end - cached_length_list
    block_len = min(512, pool_rows)
    pool_keys = cached_key_rows.reshape(pool_rows, key_local, head_dim)
    pool_values = cached_value_rows.reshape(pool_rows, key_local, head_dim)
    by_request = query_rows.reshape(
        key_local, local_requests, rows_per_request, head_dim
    ).transpose(1, 0, 2, 3)
    pool_max = maxima_over(by_request, cache_start, cache_end, pool_keys, block_len)
    top = jnp.maximum(tree_top, pool_max)
    pool_totals, pool_weighted = sums_over(
        by_request, cache_start, cache_end, top, pool_keys, pool_values, block_len
    )
    top_rows = top.transpose(1, 0, 2).reshape(key_local, token_rows * group_factor)
    tree_weights = jnp.where(tree_mask, jnp.exp(tree_scores - top_rows[:, :, None]), 0.0).astype(
        jnp.bfloat16
    )
    totals = jnp.sum(tree_weights.astype(jnp.float32), axis=2) + pool_totals.transpose(
        1, 0, 2
    ).reshape(key_local, token_rows * group_factor)
    weighted_values = jnp.einsum(
        "kqr,rkd->kqd", tree_weights, fresh_values, preferred_element_type=jnp.float32
    )
    weighted_values = weighted_values + pool_weighted.transpose(1, 0, 2, 3).reshape(
        key_local, token_rows * group_factor, head_dim
    )
    attended = (
        (weighted_values / totals[:, :, None])
        .reshape(key_local, token_rows, group_factor, head_dim)
        .transpose(1, 0, 2, 3)
    )
    attended = attended.reshape(token_rows, query_local * head_dim).astype(jnp.bfloat16)
    attend_part = jnp.dot(attended, out_weight, preferred_element_type=jnp.float32)
    share_width = model_width // vocab_shards
    share_start = vocab_shard * share_width
    residual = states + lax.psum(attend_part, "vocab")
    hidden_in = (
        residual
        * lax.rsqrt(jnp.mean(residual * residual, axis=1, keepdims=True) + eps_norm)
        * hidden_gain.astype(jnp.float32)
    ).astype(jnp.bfloat16)
    local_counts = lax.dynamic_slice_in_dim(
        live_draft_count, request_shard * local_requests, local_requests
    )
    device_totals = jnp.sum(live_draft_count.reshape(request_shards, local_requests), axis=1)
    device_ends = jnp.cumsum(device_totals)
    device_starts = device_ends - device_totals
    own_start = lax.dynamic_index_in_dim(device_starts, request_shard, keepdims=False)
    own_total = jnp.sum(local_counts)
    local_ends = jnp.cumsum(local_counts)
    local_starts = local_ends - local_counts
    token_number = jnp.arange(token_rows, dtype=jnp.int32)
    token_request = token_number // draft_length
    token_place = token_number % draft_length
    live_rows = token_place < lookup(local_counts, token_request)
    slot_count = token_rows // request_shards
    even_rows = 3 * token_rows // 4
    slot_index = jnp.arange(request_shards * slot_count, dtype=jnp.int32)
    slot_target = slot_index // slot_count
    slot_order = slot_index % slot_count * request_shards
    send_rank = slot_order + (slot_target - own_start) % request_shards
    send_request = jnp.minimum(
        jnp.sum((local_ends[None, :] <= send_rank[:, None]).astype(jnp.int32), axis=1),
        local_requests - 1,
    )
    send_row = jnp.clip(
        send_request * draft_length + send_rank - lookup(local_starts, send_request),
        0,
        token_rows - 1,
    )
    outgoing = jnp.where(
        (send_rank < own_total)[:, None],
        jnp.take(hidden_in, send_row, axis=0),
        jnp.zeros((), jnp.bfloat16),
    )
    arrived = lax.all_to_all(outgoing, "req", split_axis=0, concat_axis=0, tiled=True)
    global_rank = jnp.arange(even_rows, dtype=jnp.int32) * request_shards + request_shard
    source = jnp.minimum(
        jnp.sum((device_ends[None, :] <= global_rank[:, None]).astype(jnp.int32), axis=1),
        request_shards - 1,
    )
    source_rank = global_rank - lookup(device_starts, source)
    packed = jnp.take(arrived, source * slot_count + source_rank // request_shards, axis=0)
    computed = feed_forward(packed, gate_weight, up_weight, down_weight)
    slot_starts = lookup(device_starts, slot_target)
    return_rank = slot_order + (request_shard - slot_starts) % request_shards
    return_live = return_rank < lookup(device_totals, slot_target)
    return_row = jnp.clip((slot_starts + return_rank) // request_shards, 0, even_rows - 1)
    backward = jnp.where(
        return_live[:, None], jnp.take(computed, return_row, axis=0), jnp.zeros((), jnp.bfloat16)
    )
    returned = lax.all_to_all(backward, "req", split_axis=0, concat_axis=0, tiled=True)
    local_rank = lookup(local_starts, token_request) + token_place
    home_slot = jnp.clip(
        (own_start + local_rank) % request_shards * slot_count + local_rank // request_shards,
        0,
        request_shards * slot_count - 1,
    )
    feed_rows = jnp.take(returned, home_slot, axis=0)
    updated = jnp.where(live_rows[:, None], residual + feed_rows.astype(jnp.float32), 0.0).astype(
        jnp.bfloat16
    )
    layer_part = lax.dynamic_slice_in_dim(updated, share_start, share_width, 1)
    path_length = path_index.shape[1]
    request_picker = (
        path_index[:, :, None] == jnp.arange(draft_length, dtype=jnp.int32)[None, None, :]
    ).astype(jnp.bfloat16)
    accepted_keys = jnp.einsum(
        "ytm,ymu->ytu",
        request_picker,
        fresh_keys.reshape(local_requests, draft_length, key_local * head_dim),
        preferred_element_type=jnp.float32,
    ).astype(jnp.bfloat16)
    accepted_values = jnp.einsum(
        "ytm,ymu->ytu",
        request_picker,
        fresh_values.reshape(local_requests, draft_length, key_local * head_dim),
        preferred_element_type=jnp.float32,
    ).astype(jnp.bfloat16)
    path_states = jnp.einsum(
        "ytm,ymu->ytu",
        request_picker,
        updated.reshape(local_requests, draft_length, updated.shape[1]),
        preferred_element_type=jnp.float32,
    ).astype(jnp.bfloat16)
    per_shard = path_length // vocab_shards
    head_rows = lax.dynamic_slice_in_dim(path_states, vocab_shard * per_shard, per_shard, 1)
    flat_rows = head_rows.reshape(local_requests * per_shard, model_width).astype(jnp.float32)
    mean_square = jnp.mean(flat_rows * flat_rows, axis=1)
    norm_values = jnp.sqrt(mean_square + eps_norm).reshape(local_requests, per_shard)
    head_in = (
        flat_rows * lax.rsqrt(mean_square + eps_norm)[:, None] * final_gain.astype(jnp.float32)
    ).astype(jnp.bfloat16)
    local_max = jnp.max(
        jnp.dot(
            lax.all_gather(head_in, "req", axis=0, tiled=True),
            head_weight,
            preferred_element_type=jnp.float32,
        ),
        axis=1,
    )
    maxima = lax.pmax(local_max, "req").reshape(request_shards * local_requests, per_shard)
    return (
        layer_part.reshape(local_requests, draft_length, share_width),
        accepted_keys,
        accepted_values,
        norm_values,
        maxima,
    )


def solution(mesh):
    in_specs = (
        P("req", None, None),
        P("req", None),
        P(),
        P("req", None),
        P("req"),
        P("req", "vocab"),
        P("req", "vocab"),
        P(),
        P(),
        P(),
        P(None, "vocab"),
        P(None, "vocab"),
        P(None, "vocab"),
        P("vocab", None),
        P(None, "vocab"),
        P(None, "vocab"),
        P("vocab", None),
        P(None, "req"),
    )
    out_specs = (
        P("req", None, "vocab"),
        P("req", None, "vocab"),
        P("req", None, "vocab"),
        P("req", "vocab"),
        P(None, "vocab"),
    )
    return jax.shard_map(
        per_device, mesh=mesh, in_specs=in_specs, out_specs=out_specs, check_vma=False
    )
```

profile of v0, /device:TPU:6, one launch (start us, length us, event | category | flops | bytes accessed | tf_op | source)
XLA Modules:
  0.0 430.9 jit_solution(2715974961499457239)
XLA Ops:
  7.8 1.4 reduce-window.24
  9.2 1.3 bitcast_subtract_fusion.3
  10.4 1.2 fusion.28
  12.9 1.0 convolution_minimum_fusion.5
  17.1 0.9 gt.15
  18.8 1.4 copy.72
  21.9 1.4 fusion.105
  25.5 1.6 maximum_bitcast_fusion
  27.1 14.0 %while.104 = (s32[]{:T(128)}, f32[2,1,128]{2,1,0:T(1,128)S(1)}, s32[2]{0:T(128)}, s32[2]{0:T(128)}, bf16[2,1,128,96]{3,2,1,0:T(8,128)(2,1)}, /*index=5*/bf16[204...) while((s32[]{:T(128)}, f32[2,1,128]{2,1,0:T(1,128)S(1)}, ...), condition=%wide.region_9.10_spmd, body=%wide.region_5.9_spmd.sunk | while | flops 12781597 | bytes 177346 | solution.py:94
  27.1 1.2 dynamic_slice.135
  28.4 1.3 dynamic_slice.136
  31.6 2.5 while.107
  32.8 1.2 fusion.151
  34.1 1.2 dynamic_slice.135
  35.4 1.3 dynamic_slice.136
  38.6 2.5 while.107
  39.8 1.2 fusion.151
  41.4 1.8 convolution_convert_fusion.1
  43.7 0.9 select_reduce_fusion
  44.6 27.5 %while.106 = (s32[]{:T(128)}, f32[2,1,128]{2,1,0:T(1,128)S(1)}, f32[2,1,128,96]{2,0,3,1:T(2,128)}, s32[2]{0:T(128)}, s32[2]{0:T(128)}, /*index=5*/bf16[2,1,128,9...) while((s32[]{:T(128)}, f32[2,1,128]{2,1,0:T(1,128)S(1)}, ...), condition=%wide.region_14.15_spmd, body=%wide.region_10.14_spmd.sunk | while | flops 25573404 | bytes 785178 | solution.py:101
  44.6 1.2 dynamic_slice.139
  45.9 1.3 dynamic_slice.140
  50.2 4.8 %while.108 = (s32[]{:T(128)}, f32[1,128]{1,0:T(1,128)}, f32[1,128,96]{1,2,0:T(8,128)S(1)}, s32[]{:T(128)}, s32[]{:T(128)}, /*index=5*/s32[]{:T(128)}, bf16[2048,...) while((s32[]{:T(128)}, f32[1,128]{1,0:T(1,128)}, ...), condition=%wide.region_13.13_spmd, body=%wide.region_11.12_spmd.sunk | while | flops 25573384 | bytes 585471 | solution.py:90
  51.4 1.3 convert_reduce_fusion.4
  52.7 1.2 bitcast_add_fusion.4
  53.9 1.1 fusion.147
  55.7 2.7 dynamic_update_slice.39
  58.4 1.2 dynamic_slice.139
  59.6 1.3 dynamic_slice.140
  63.9 4.8 %while.108 = (s32[]{:T(128)}, f32[1,128]{1,0:T(1,128)}, f32[1,128,96]{1,2,0:T(8,128)S(1)}, s32[]{:T(128)}, s32[]{:T(128)}, /*index=5*/s32[]{:T(128)}, bf16[2048,...) while((s32[]{:T(128)}, f32[1,128]{1,0:T(1,128)}, ...), condition=%wide.region_13.13_spmd, body=%wide.region_11.12_spmd.sunk | while | flops 25573384 | bytes 585471 | solution.py:90
  65.2 1.3 convert_reduce_fusion.4
  66.4 1.2 bitcast_add_fusion.4
  67.6 1.1 fusion.147
  69.4 2.7 dynamic_update_slice.39
  72.1 1.0 convert_reduce_fusion.1
  73.1 1.2 fusion.27
  75.0 0.9 convert_element_type.152
  75.9 2.2 fusion.106
  81.7 1.3 compare_and_fusion.2
  83.4 83.3 %all-reduce.3.cloned.1.call-done = f32[128,1536]{1,0:T(8,128)} async-done(((f32[128,1536]{1,0:T(8,128)}), f32[128,1536]{1,0:T(8,128)}) %all-reduce.3.cloned.1.call-update) | async-done | bytes 786448 | tf_op jit(solution)/shard_map/psum | solution.py:229
  166.7 1.4 multiply_reduce_fusion
  168.1 1.1 multiply_convert_fusion
  169.3 1.6 gather_fusion.2
  170.9 1.1 select_select_fusion
  172.9 10.0 %all-to-all-start = ((bf16[32,4,1536]{2,1,0:T(4,128)(2,1)}), bf16[32,4,1536]{2,1,0:T(4,128)(2,1)}, u32[]{:S(2)}, u32[]{:S(2)}) async-start(bf16[32,4,1536]{2,1,0:T(4,128)(2,1)} %all_to_all.14), calls=%async_computation | async-start | bytes 786432 | tf_op jit(solution)/shard_map/all_to_all | solution.py:269
  183.1 15.1 %all-to-all-done = bf16[32,4,1536]{2,1,0:T(4,128)(2,1)} async-done(((bf16[32,4,1536]{2,1,0:T(4,128)(2,1)}), bf16[32,4,1536]{2,1,0:T(4,128)(2,1)}, u32[]{:S(2)}, u32[]{:S(2)}) %all-to-all-start) | async-done | bytes 393248 | tf_op jit(solution)/shard_map/all_to_all | solution.py:269
  198.1 1.1 all_to_all.16
  199.2 1.5 gather_fusion
  200.7 2.7 fusion.38
  203.4 3.5 convolution_convert_fusion
  208.0 58.5 %all-reduce.5.cloned.1.call-done = bf16[96,1536]{1,0:T(8,128)(2,1)} async-done(((bf16[96,1536]{1,0:T(8,128)(2,1)}), bf16[96,1536]{1,0:T(8,128)(2,1)}) %all-reduce.5.cloned.1.call-update) | async-done | bytes 294928 | tf_op jit(solution)/shard_map/psum | solution.py:114
  266.5 3.0 gather_fusion.1
  269.5 1.1 gather.15
  270.6 1.2 select_select_fusion.1
  271.8 10.0 %all-to-all-start.1 = ((bf16[32,4,1536]{2,1,0:T(4,128)(2,1)}), bf16[32,4,1536]{2,1,0:T(4,128)(2,1)}, u32[]{:S(2)}, u32[]{:S(2)}) async-start(bf16[32,4,1536]{2,1,0:T(4,128)(2,1)} %select_select_fusion.1), calls=%async_computation.1 | async-start | bytes 786432 | tf_op jit(solution)/shard_map/all_to_all | solution.py:285
  281.7 1.3 compare_and_fusion.1
  283.9 1.5 convolution_convert_fusion.2
  285.4 12.0 %all-to-all-done.1 = bf16[32,4,1536]{2,1,0:T(4,128)(2,1)} async-done(((bf16[32,4,1536]{2,1,0:T(4,128)(2,1)}), bf16[32,4,1536]{2,1,0:T(4,128)(2,1)}, u32[]{:S(2)}, u32[]{:S(2)}) %all-to-all-start.1) | async-done | bytes 393248 | tf_op jit(solution)/shard_map/all_to_all | solution.py:285
  297.4 1.1 all_to_all.18
  298.5 1.6 gather_fusion.3
  300.2 1.6 select_convert_fusion
  303.5 46.6 %all-gather = bf16[32,2,1536]{2,1,0:T(2,128)(2,1)S(1)} all-gather(bf16[1,2,1536]{2,1,0:T(2,128)(2,1)S(1)} %fusion.76), channel_id=1, replica_groups=mesh['req'=32,'vocab'=8] {'req'}, dimensions={0}, use_global_device_ids=true | all-gather | bytes 202752 | tf_op jit(solution)/shard_map/all_gather | solution.py:329
  350.2 1.1 convolution_reduce_fusion
  351.3 72.8 %pmax.7 = f32[64,1]{0,1:T(1,128)} all-reduce(f32[64,1]{0,1:T(1,128)S(1)} %bitcast.225), channel_id=1, replica_groups=mesh['req'=32,'vocab'=8] {'req'}, use_global_device_ids=true, to_apply=%region_32.34 | all-reduce | flops 64 | bytes 512 | tf_op jit(solution)/shard_map/pmax | solution.py:335
  (150 shorter events, 26.1 us)
Async XLA Ops:
  7.2 343.0 %copy-start = (bf16[1536,1000]{0,1:T(8,128)(2,1)S(1)}, bf16[1536,1000]{0,1:T(8,128)(2,1)}, u32[]{:S(2)}) copy-start(bf16[1536,1000]{0,1:T(8,128)(2,1)} %param.45) | copy-start | bytes 9216004
  7.2 13.1 %copy-start.1 = (bf16[2,64,1536]{2,1,0:T(8,128)(2,1)S(1)}, bf16[2,64,1536]{2,1,0:T(8,128)(2,1)}, u32[]{:S(2)}) copy-start(bf16[2,64,1536]{2,1,0:T(8,128)(2,1)} %param.28) | copy-start | bytes 1179652
  7.2 159.5 %all-reduce.3.cloned.1.call-start = ((), (), s32[]{:S(2)}) async-start(), calls=%async_computation.2 | async-start | bytes 1572864 | tf_op jit(solution)/shard_map/psum | solution.py:229
  11.6 2.9 copy-start.17
  12.9 10.4 %copy-start.14 = (f32[1536]{0:T(1024)}, f32[1536]{0:T(1024)S(1)}, u32[]{:S(2)}) copy-start(f32[1536]{0:T(1024)S(1)} %convert_element_type.141) | copy-start | bytes 18436
  24.8 2.3 copy-start.4
  27.1 14.0 %copy-start.15 = (f32[1536]{0:T(1024)S(1)}, f32[1536]{0:T(1024)}, u32[]{:S(2)}) copy-start(f32[1536]{0:T(1024)} %copy-done.14) | copy-start | bytes 18436
  27.1 14.0 %copy-start.23 = (f32[128]{0:T(128)S(1)}, f32[128]{0:T(128)}, u32[]{:S(2)}) copy-start(f32[128]{0:T(128)} %rsqrt.28) | copy-start | bytes 1540
  41.1 2.1 copy-start.8
  41.1 2.3 copy-start.20
  41.2 2.3 copy-start.21
  41.2 2.5 copy-start.5
  41.2 2.5 copy-start.6
  41.2 2.5 copy-start.7
  43.6 1.0 copy-start.9
  43.7 0.9 copy-start.11
  72.1 6.1 %copy-start.22 = (s32[64]{0:T(128)S(1)}, s32[64]{0:T(128)}, u32[]{:S(2)}) copy-start(s32[64]{0:T(128)} %param.30) | copy-start | bytes 772
  73.1 10.0 %copy-start.18 = (bf16[1536]{0:T(1024)(128)(2,1)S(1)}, bf16[1536]{0:T(1024)(128)(2,1)}, u32[]{:S(2)}) copy-start(bf16[1536]{0:T(1024)(128)(2,1)} %param.36) | copy-start | bytes 9220
  166.7 1.4 copy-start.2
  172.9 25.2 %all-to-all-start = ((bf16[32,4,1536]{2,1,0:T(4,128)(2,1)}), bf16[32,4,1536]{2,1,0:T(4,128)(2,1)}, u32[]{:S(2)}, u32[]{:S(2)}) async-start(bf16[32,4,1536]{2,1,0:T(4,128)(2,1)} %all_to_all.14), calls=%async_computation | async-start | bytes 786432 | tf_op jit(solution)/shard_map/all_to_all | solution.py:269
  182.9 83.6 %all-reduce.5.cloned.1.call-start = ((), (), s32[]{:S(2)}) async-start(), calls=%async_computation.3 | async-start | bytes 589824 | tf_op jit(solution)/shard_map/psum | solution.py:114
  200.7 2.7 copy-start.3
  203.4 3.6 copy-start.13
  203.4 4.3 %copy-start.12 = (bf16[128,1,48]{0,2,1:T(8,128)(2,1)S(1)}, bf16[128,1,48]{0,2,1:T(8,128)(2,1)}, u32[]{:S(2)}) copy-start(bf16[128,1,48]{0,2,1:T(8,128)(2,1)} %copy-done.11) | copy-start | bytes 36868
  203.4 4.4 %copy-start.10 = (bf16[128,1,48]{0,2,1:T(8,128)(2,1)S(1)}, bf16[128,1,48]{0,2,1:T(8,128)(2,1)}, u32[]{:S(2)}) copy-start(bf16[128,1,48]{0,2,1:T(8,128)(2,1)} %copy-done.9) | copy-start | bytes 36868
  203.4 4.6 %copy-start.19 = (bf16[1536]{0:T(1024)(128)(2,1)S(1)}, bf16[1536]{0:T(1024)(128)(2,1)}, u32[]{:S(2)}) copy-start(bf16[1536]{0:T(1024)(128)(2,1)} %param.37) | copy-start | bytes 9220
  269.5 13.6 %copy-start.16 = (s32[2,8]{1,0:T(2,128)S(1)}, s32[2,8]{1,0:T(2,128)}, u32[]{:S(2)}) copy-start(s32[2,8]{1,0:T(2,128)} %param.31) | copy-start | bytes 196
  271.8 25.7 %all-to-all-start.1 = ((bf16[32,4,1536]{2,1,0:T(4,128)(2,1)}), bf16[32,4,1536]{2,1,0:T(4,128)(2,1)}, u32[]{:S(2)}, u32[]{:S(2)}) async-start(bf16[32,4,1536]{2,1,0:T(4,128)(2,1)} %select_select_fusion.1), calls=%async_computation.1 | async-start | bytes 786432 | tf_op jit(solution)/shard_map/all_to_all | solution.py:285
Sparse Core Ops, SparseCore 0:
  78.3 88.3 all-reduce.2
  207.1 59.3 all-reduce.4
where the time goes:
time: 433 us; the launch traced here: 431 us
  waiting for transfers between devices  169 us (39%)
  blocking collectives  119 us (27%)
  local copies, waits for them, and re-layouts  44.3 us (10%)
  other arithmetic  26.9 us (6%)
  matrix products  26.9 us (6%)
  starting transfers between devices  20 us (5%)
  between operations  14.6 us (3%)
  loops' own time  9.85 us (2%)
    psum x1, waiting for transfers between devices, per_device(): residual = states + lax.psum(attend_part, 'vocab')  83.3 us
    pmax x1, blocking collectives, per_device(): lax.pmax(local_max, 'req')  72.8 us
    psum x1, waiting for transfers between devices, feed_forward(): summed = lax.psum(partial_sum.astype(jnp.bfloat16), 'vocab')  58.5 us
    all_gather x1, blocking collectives, per_device(): lax.all_gather(head_in, 'req', axis=0, tiled=True)  46.6 us
    all_to_all x1, waiting for transfers between devices, per_device(): lax.all_to_all(outgoing, 'req', split_axis=0, concat_axis=0, tiled=True)  15.1 us
    all_to_all x1, waiting for transfers between devices, per_device(): lax.all_to_all(backward, 'req', split_axis=0, concat_axis=0, tiled=True)  12 us
    dynamic_slice x8, local copies, waits for them, and re-layouts, maxima_over(): lax.map(lambda item: span_max(item[0], item[1], item[2], joined_keys, blo...  10 us
    all_to_all x1, starting transfers between devices, per_device(): lax.all_to_all(backward, 'req', split_axis=0, concat_axis=0, tiled=True)  9.96 us
  transfers between devices with their start and end apart: 4, of which 4 were waited for; matrix products, arithmetic and copies ran while one was open for 2% of the time, Pallas kernels for 0%

commit v1 on v0

--- a/solution.py
+++ b/solution.py
@@ -111,7 +111,7 @@
     up_out = jnp.dot(hidden_in, up_weight, preferred_element_type=jnp.float32)
     hidden = (jax.nn.silu(gate_out) * up_out).astype(jnp.bfloat16)
     partial_sum = jnp.dot(hidden, down_weight, preferred_element_type=jnp.float32)
-    summed = lax.psum(partial_sum.astype(jnp.bfloat16), "vocab")
+    summed = jnp.sum(lax.all_gather(partial_sum.astype(jnp.bfloat16), "vocab"), axis=0)
     return summed
 
 

time: 433 us -> 398 us (0.919)
  waiting for transfers between devices: 169 us -> 132 us
    psum x1 -> x0, waiting for transfers between devices: 58.5 us -> none  [feed_forward(): summed = lax.psum(partial_sum.astype(jnp.bfloat16), 'vocab')]
    all_gather x0 -> x1, waiting for transfers between devices: none -> 22.6 us  [feed_forward(): lax.all_gather(partial_sum.astype(jnp.bfloat16), 'vocab')]
where the time goes in v1:
time: 398 us; the launch traced here: 395 us
  waiting for transfers between devices  132 us (33%)
  blocking collectives  120 us (30%)
  local copies, waits for them, and re-layouts  42.9 us (11%)
  other arithmetic  28.9 us (7%)
  matrix products  26.9 us (7%)
  starting transfers between devices  20 us (5%)
  between operations  14.6 us (4%)
  loops' own time  9.85 us (2%)
    psum x1, waiting for transfers between devices, per_device(): residual = states + lax.psum(attend_part, 'vocab')  83.7 us
    pmax x1, blocking collectives, per_device(): lax.pmax(local_max, 'req')  72.8 us
    all_gather x1, blocking collectives, per_device(): lax.all_gather(head_in, 'req', axis=0, tiled=True)  47.1 us
    all_gather x1, waiting for transfers between devices, feed_forward(): lax.all_gather(partial_sum.astype(jnp.bfloat16), 'vocab')  22.6 us
    all_to_all x1, waiting for transfers between devices, per_device(): lax.all_to_all(outgoing, 'req', split_axis=0, concat_axis=0, tiled=True)  15 us
    all_to_all x1, waiting for transfers between devices, per_device(): lax.all_to_all(backward, 'req', split_axis=0, concat_axis=0, tiled=True)  10.7 us
    dynamic_slice x8, local copies, waits for them, and re-layouts, maxima_over(): lax.map(lambda item: span_max(item[0], item[1], item[2], joined_keys, blo...  10 us
    all_to_all x1, starting transfers between devices, per_device(): lax.all_to_all(backward, 'req', split_axis=0, concat_axis=0, tiled=True)  9.96 us
  transfers between devices with their start and end apart: 4, of which 4 were waited for; matrix products, arithmetic and copies ran while one was open for 2% of the time, Pallas kernels for 0%

profile of v1, /device:TPU:6, one launch (start us, length us, event | category | flops | bytes accessed | tf_op | source)
XLA Modules:
  0.0 395.2 jit_solution(8013796173126080211)
XLA Ops:
  7.8 1.4 reduce-window.24
  9.2 1.3 bitcast_subtract_fusion.3
  10.4 1.2 fusion.28
  12.9 1.0 convolution_minimum_fusion.5
  17.1 0.9 gt.15
  18.8 1.4 copy.72
  21.9 1.4 fusion.105
  25.5 1.6 maximum_bitcast_fusion
  27.1 14.0 %while.104 = (s32[]{:T(128)}, f32[2,1,128]{2,1,0:T(1,128)S(1)}, s32[2]{0:T(128)}, s32[2]{0:T(128)}, bf16[2,1,128,96]{3,2,1,0:T(8,128)(2,1)}, /*index=5*/bf16[204...) while((s32[]{:T(128)}, f32[2,1,128]{2,1,0:T(1,128)S(1)}, ...), condition=%wide.region_9.10_spmd, body=%wide.region_5.9_spmd.sunk | while | flops 12781597 | bytes 177346 | solution.py:94
  27.1 1.2 dynamic_slice.135
  28.4 1.3 dynamic_slice.136
  31.6 2.5 while.107
  32.8 1.2 fusion.151
  34.1 1.2 dynamic_slice.135
  35.4 1.3 dynamic_slice.136
  38.6 2.5 while.107
  39.8 1.2 fusion.151
  41.4 1.8 convolution_convert_fusion.1
  44.6 27.5 %while.106 = (s32[]{:T(128)}, f32[2,1,128]{2,1,0:T(1,128)S(1)}, f32[2,1,128,96]{2,0,3,1:T(2,128)}, s32[2]{0:T(128)}, s32[2]{0:T(128)}, /*index=5*/bf16[2,1,128,9...) while((s32[]{:T(128)}, f32[2,1,128]{2,1,0:T(1,128)S(1)}, ...), condition=%wide.region_14.15_spmd, body=%wide.region_10.14_spmd.sunk | while | flops 25573404 | bytes 785178 | solution.py:101
  44.6 1.2 dynamic_slice.139
  45.9 1.3 dynamic_slice.140
  50.2 4.8 %while.108 = (s32[]{:T(128)}, f32[1,128]{1,0:T(1,128)}, f32[1,128,96]{1,2,0:T(8,128)S(1)}, s32[]{:T(128)}, s32[]{:T(128)}, /*index=5*/s32[]{:T(128)}, bf16[2048,...) while((s32[]{:T(128)}, f32[1,128]{1,0:T(1,128)}, ...), condition=%wide.region_13.13_spmd, body=%wide.region_11.12_spmd.sunk | while | flops 25573384 | bytes 585471 | solution.py:90
  51.4 1.3 convert_reduce_fusion.4
  52.7 1.2 bitcast_add_fusion.4
  53.9 1.1 fusion.147
  55.7 2.7 dynamic_update_slice.39
  58.4 1.2 dynamic_slice.139
  59.6 1.3 dynamic_slice.140
  63.9 4.8 %while.108 = (s32[]{:T(128)}, f32[1,128]{1,0:T(1,128)}, f32[1,128,96]{1,2,0:T(8,128)S(1)}, s32[]{:T(128)}, s32[]{:T(128)}, /*index=5*/s32[]{:T(128)}, bf16[2048,...) while((s32[]{:T(128)}, f32[1,128]{1,0:T(1,128)}, ...), condition=%wide.region_13.13_spmd, body=%wide.region_11.12_spmd.sunk | while | flops 25573384 | bytes 585471 | solution.py:90
  65.2 1.3 convert_reduce_fusion.4
  66.4 1.2 bitcast_add_fusion.4
  67.6 1.1 fusion.147
  69.4 2.7 dynamic_update_slice.39
  72.1 1.0 convert_reduce_fusion.1
  73.1 1.2 fusion.27
  75.0 0.9 convert_element_type.154
  75.9 2.2 fusion.106
  81.5 1.3 compare_and_fusion.2
  83.0 83.7 %all-reduce.2.cloned.1.call-done = f32[128,1536]{1,0:T(8,128)} async-done(((f32[128,1536]{1,0:T(8,128)}), f32[128,1536]{1,0:T(8,128)}) %all-reduce.2.cloned.1.call-update) | async-done | bytes 786448 | tf_op jit(solution)/shard_map/psum | solution.py:229
  166.7 1.4 multiply_reduce_fusion
  168.1 1.1 multiply_convert_fusion
  169.3 1.6 gather_fusion.2
  170.9 1.1 select_select_fusion
  172.9 10.0 %all-to-all-start = ((bf16[32,4,1536]{2,1,0:T(4,128)(2,1)}), bf16[32,4,1536]{2,1,0:T(4,128)(2,1)}, u32[]{:S(2)}, u32[]{:S(2)}) async-start(bf16[32,4,1536]{2,1,0:T(4,128)(2,1)} %all_to_all.14), calls=%async_computation | async-start | bytes 786432 | tf_op jit(solution)/shard_map/all_to_all | solution.py:269
  183.1 15.0 %all-to-all-done = bf16[32,4,1536]{2,1,0:T(4,128)(2,1)} async-done(((bf16[32,4,1536]{2,1,0:T(4,128)(2,1)}), bf16[32,4,1536]{2,1,0:T(4,128)(2,1)}, u32[]{:S(2)}, u32[]{:S(2)}) %all-to-all-start) | async-done | bytes 393248 | tf_op jit(solution)/shard_map/all_to_all | solution.py:269
  198.1 1.1 all_to_all.16
  199.1 1.5 gather_fusion
  200.7 2.6 fusion.38
  203.3 3.5 convolution_convert_fusion
  208.3 22.6 %all-gather.4.cloned.1.call-done = bf16[768,1536]{1,0:T(8,128)(2,1)} async-done(((bf16[96,1536]{1,0:T(8,128)(2,1)}), bf16[768,1536]{1,0:T(8,128)(2,1)}) %all-gather.4.cloned.1.call-update) | async-done | bytes 2359312 | tf_op jit(solution)/shard_map/all_gather | solution.py:114
  230.9 2.0 reduce_sum.182
  233.0 1.6 gather_fusion.1
  234.6 1.1 gather.15
  235.7 1.1 select_select_fusion.1
  236.8 10.0 %all-to-all-start.1 = ((bf16[32,4,1536]{2,1,0:T(4,128)(2,1)}), bf16[32,4,1536]{2,1,0:T(4,128)(2,1)}, u32[]{:S(2)}, u32[]{:S(2)}) async-start(bf16[32,4,1536]{2,1,0:T(4,128)(2,1)} %select_select_fusion.1), calls=%async_computation.1 | async-start | bytes 786432 | tf_op jit(solution)/shard_map/all_to_all | solution.py:285
  246.8 1.3 compare_and_fusion.1
  249.0 1.5 convolution_convert_fusion.2
  250.5 10.7 %all-to-all-done.1 = bf16[32,4,1536]{2,1,0:T(4,128)(2,1)} async-done(((bf16[32,4,1536]{2,1,0:T(4,128)(2,1)}), bf16[32,4,1536]{2,1,0:T(4,128)(2,1)}, u32[]{:S(2)}, u32[]{:S(2)}) %all-to-all-start.1) | async-done | bytes 393248 | tf_op jit(solution)/shard_map/all_to_all | solution.py:285
  261.3 1.1 all_to_all.18
  262.3 1.6 gather_fusion.3
  264.0 1.6 select_convert_fusion
  267.3 47.1 %all-gather.1 = bf16[32,2,1536]{2,1,0:T(2,128)(2,1)S(1)} all-gather(bf16[1,2,1536]{2,1,0:T(2,128)(2,1)S(1)} %fusion.76), channel_id=1, replica_groups=mesh['req'=32,'vocab'=8] {'req'}, dimensions={0}, use_global_device_ids=true | all-gather | bytes 202752 | tf_op jit(solution)/shard_map/all_gather | solution.py:329
  314.5 1.1 convolution_reduce_fusion
  315.6 72.8 %pmax.7 = f32[64,1]{0,1:T(1,128)} all-reduce(f32[64,1]{0,1:T(1,128)S(1)} %bitcast.227), channel_id=1, replica_groups=mesh['req'=32,'vocab'=8] {'req'}, use_global_device_ids=true, to_apply=%region_32.34 | all-reduce | flops 64 | bytes 512 | tf_op jit(solution)/shard_map/pmax | solution.py:335
  (151 shorter events, 26.9 us)
Async XLA Ops:
  7.2 307.3 %copy-start = (bf16[1536,1000]{0,1:T(8,128)(2,1)S(1)}, bf16[1536,1000]{0,1:T(8,128)(2,1)}, u32[]{:S(2)}) copy-start(bf16[1536,1000]{0,1:T(8,128)(2,1)} %param.45) | copy-start | bytes 9216004
  7.2 13.1 %copy-start.1 = (bf16[2,64,1536]{2,1,0:T(8,128)(2,1)S(1)}, bf16[2,64,1536]{2,1,0:T(8,128)(2,1)}, u32[]{:S(2)}) copy-start(bf16[2,64,1536]{2,1,0:T(8,128)(2,1)} %param.28) | copy-start | bytes 1179652
  7.2 159.5 %all-reduce.2.cloned.1.call-start = ((), (), s32[]{:S(2)}) async-start(), calls=%async_computation.2 | async-start | bytes 1572864 | tf_op jit(solution)/shard_map/psum | solution.py:229
  11.6 2.9 copy-start.17
  12.9 10.4 %copy-start.14 = (f32[1536]{0:T(1024)}, f32[1536]{0:T(1024)S(1)}, u32[]{:S(2)}) copy-start(f32[1536]{0:T(1024)S(1)} %convert_element_type.143) | copy-start | bytes 18436
  24.8 2.3 copy-start.4
  27.1 14.0 %copy-start.15 = (f32[1536]{0:T(1024)S(1)}, f32[1536]{0:T(1024)}, u32[]{:S(2)}) copy-start(f32[1536]{0:T(1024)} %copy-done.14) | copy-start | bytes 18436
  27.1 14.0 %copy-start.23 = (f32[128]{0:T(128)S(1)}, f32[128]{0:T(128)}, u32[]{:S(2)}) copy-start(f32[128]{0:T(128)} %rsqrt.28) | copy-start | bytes 1540
  41.1 2.1 copy-start.8
  41.1 2.3 copy-start.20
  41.2 2.3 copy-start.21
  41.2 2.5 copy-start.5
  41.2 2.5 copy-start.6
  41.2 2.5 copy-start.7
  43.6 1.0 copy-start.9
  43.7 0.9 copy-start.11
  72.1 6.1 %copy-start.22 = (s32[64]{0:T(128)S(1)}, s32[64]{0:T(128)}, u32[]{:S(2)}) copy-start(s32[64]{0:T(128)} %param.30) | copy-start | bytes 772
  73.1 9.8 %copy-start.18 = (bf16[1536]{0:T(1024)(128)(2,1)S(1)}, bf16[1536]{0:T(1024)(128)(2,1)}, u32[]{:S(2)}) copy-start(bf16[1536]{0:T(1024)(128)(2,1)} %param.36) | copy-start | bytes 9220
  166.7 1.4 copy-start.2
  172.9 25.2 %all-to-all-start = ((bf16[32,4,1536]{2,1,0:T(4,128)(2,1)}), bf16[32,4,1536]{2,1,0:T(4,128)(2,1)}, u32[]{:S(2)}, u32[]{:S(2)}) async-start(bf16[32,4,1536]{2,1,0:T(4,128)(2,1)} %all_to_all.14), calls=%async_computation | async-start | bytes 786432 | tf_op jit(solution)/shard_map/all_to_all | solution.py:269
  182.8 48.1 %all-gather.4.cloned.1.call-start = ((), (), s32[]{:S(2)}) async-start(), calls=%async_computation.3 | async-start | bytes 2654208 | tf_op jit(solution)/shard_map/all_gather | solution.py:114
  200.7 2.6 copy-start.3
  203.3 3.6 copy-start.13
  203.3 4.3 %copy-start.12 = (bf16[128,1,48]{0,2,1:T(8,128)(2,1)S(1)}, bf16[128,1,48]{0,2,1:T(8,128)(2,1)}, u32[]{:S(2)}) copy-start(bf16[128,1,48]{0,2,1:T(8,128)(2,1)} %copy-done.11) | copy-start | bytes 36868
  203.3 4.4 %copy-start.10 = (bf16[128,1,48]{0,2,1:T(8,128)(2,1)S(1)}, bf16[128,1,48]{0,2,1:T(8,128)(2,1)}, u32[]{:S(2)}) copy-start(bf16[128,1,48]{0,2,1:T(8,128)(2,1)} %copy-done.9) | copy-start | bytes 36868
  203.3 4.5 %copy-start.19 = (bf16[1536]{0:T(1024)(128)(2,1)S(1)}, bf16[1536]{0:T(1024)(128)(2,1)}, u32[]{:S(2)}) copy-start(bf16[1536]{0:T(1024)(128)(2,1)} %param.37) | copy-start | bytes 9220
  234.6 13.6 %copy-start.16 = (s32[2,8]{1,0:T(2,128)S(1)}, s32[2,8]{1,0:T(2,128)}, u32[]{:S(2)}) copy-start(s32[2,8]{1,0:T(2,128)} %param.31) | copy-start | bytes 196
  236.8 24.4 %all-to-all-start.1 = ((bf16[32,4,1536]{2,1,0:T(4,128)(2,1)}), bf16[32,4,1536]{2,1,0:T(4,128)(2,1)}, u32[]{:S(2)}, u32[]{:S(2)}) async-start(bf16[32,4,1536]{2,1,0:T(4,128)(2,1)} %select_select_fusion.1), calls=%async_computation.1 | async-start | bytes 786432 | tf_op jit(solution)/shard_map/all_to_all | solution.py:285
Sparse Core Ops, SparseCore 0:
  78.3 88.3 all-reduce.1
  207.0 23.8 all-gather.3
